TPU v7x, 128 devices: a whole 4x4x4 slice. The times are simulated.
128 devices in a mesh: space: 32 (over y, x, core), shell: 4 (over z).
Axes of the slice: x: 4, y: 4, z: 4, core: 2. Of those that a mesh axis runs over, the one named last changes fastest.
Arguments:
- weights: float32 [262144], P(('space', 'shell')), may hold values from 0.02 to 1.5
- seg_streamline: int32 [32, 4, 32, 256], P('space', 'shell'), may hold values from 0 to 2047
- seg_features: float32 [32, 4, 32, 256, 128], P('space', 'shell'), may hold values from -12 to 12
- pair_counts: int32 [32, 4, 32], P('space', 'shell'), may hold values from 32 to 256, as said below
- seg_voxel: int32 [32, 4, 32, 256], P('space', 'shell'), may hold values from 0 to 4095
- dictionary: float32 [128, 256], P(None, 'shell'), may hold values from -0.375 to 0.375
- measured: float32 [256, 131072], P('shell', 'space'), may hold values from -6 to 6
Outputs:
- new_weights: float32 [262144], P(('space', 'shell'))
- residual: float32 [256, 131072], P('shell', 'space')
Inputs may be any that keep to these rules, and one draw needn't show every extreme that they name: In each shell group q one voxel block d has pair_counts[s, q, d] = 256 for every s.
All inputs are finite; a program needn't handle non-finite values.
Results may differ from a plain program's by a relative error of at most 0.0003.
Values sent between devices are 32-bit elements; how exact they have to be, the bound alone decides.
No kernel may reach another device: no remote copies, remote signals or barrier semaphores. Data moves between devices by JAX's collectives and lax.ppermute only.
A program may use at most 64 MiB of HBM per device.

v0:
```python
import jax
import jax.numpy as jnp
from jax import lax
from jax.sharding import PartitionSpec as P

ITERS = 2


def on_device(weights, seg_streamline, seg_features, pair_counts, seg_voxel, dictionary, measured):
    blocks = seg_streamline.shape[2]
    slots = seg_streamline.shape[3]
    coeffs = seg_features.shape[4]
    voxel_count = measured.shape[1]
    stream_index = seg_streamline.reshape(blocks, slots)
    voxel_index = seg_voxel.reshape(blocks * slots)
    counts = pair_counts.reshape(blocks)
    live_slot = lax.broadcasted_iota(jnp.int32, (blocks, slots), 1) < counts[:, None]
    masked = jnp.where(
        live_slot[:, :, None], seg_features.reshape(blocks, slots, coeffs), jnp.float32(0.0)
    )
    column_sq = (
        jnp.zeros(weights.shape, jnp.float32).at[stream_index].add(jnp.sum(masked * masked, axis=2))
    )
    scaling = 0.5 / (0.5 + column_sq)
    current = weights
    residual = jnp.zeros(measured.shape, jnp.float32)
    for iteration in range(ITERS):
        picked = current[stream_index]
        seg_terms = lax.all_to_all(
            picked[:, :, None] * masked, "space", split_axis=0, concat_axis=0, tiled=True
        )
        partial_coeff = (
            jnp.zeros((voxel_count, coeffs), jnp.float32)
            .at[voxel_index]
            .add(seg_terms.reshape(blocks * slots, coeffs))
        )
        coeff_sum = lax.psum(partial_coeff, "shell")
        residual = (
            jnp.einsum("jg,vj->gv", dictionary, coeff_sum, precision=lax.Precision.HIGHEST)
            - measured
        )
        adjoint = lax.psum(
            jnp.einsum("gv,jg->vj", residual, dictionary, precision=lax.Precision.HIGHEST), "shell"
        )
        adj_rows = adjoint[voxel_index].reshape(blocks, slots, coeffs)
        grad_slot = jnp.sum(
            masked * lax.all_to_all(adj_rows, "space", split_axis=0, concat_axis=0, tiled=True),
            axis=2,
        )
        gradient = jnp.zeros(weights.shape, jnp.float32).at[stream_index].add(grad_slot)
        current = jnp.maximum(current - scaling * gradient, 0.0)
    return (current, residual)


def solution(mesh):
    in_specs = (
        P(("space", "shell")),
        P("space", "shell", None, None),
        P("space", "shell", None, None, None),
        P("space", "shell", None),
        P("space", "shell", None, None),
        P(None, "shell"),
        P("shell", "space"),
    )
    out_specs = (P(("space", "shell")), P("shell", "space"))
    return jax.shard_map(
        on_device, mesh=mesh, in_specs=in_specs, out_specs=out_specs, check_vma=False
    )
```

profile of v0, /device:TPU:1, one launch (start us, length us, event | category | flops | bytes accessed | tf_op | source)
XLA Modules:
  0.0 890.2 jit_solution(17388944566047050254)
XLA Ops:
  7.2 0.0 copy-start
  7.2 0.0 copy-start.1
  7.2 0.7 iota_compare_fusion
  7.9 0.8 fusion.8
  8.7 0.0 copy-done.1
  8.7 45.5 %gather_fusion = f32[8192]{0:T(1024)S(1)} fusion(f32[2048]{0:T(1024)S(1)} %copy-done.1, s32[8192]{0:T(1024)S(1)} %broadcast_clamp_fusion.1), kind=kCustom, calls=%fused_computation | custom fusion | bytes 98304 | tf_op jit(solution)/shard_map/gather | solution.py:28
  54.3 7.7 fusion.3
  62.0 0.0 copy-start.6
  62.0 8.8 all-to-all-start
  70.7 0.0 copy-start.5
  70.8 0.0 all-reduce.5.cloned.1.call-start
  70.8 0.0 copy-done.6
  70.9 50.1 %all-to-all-done = f32[32,256,128]{2,1,0:T(8,128)} async-done(((f32[32,256,128]{2,1,0:T(8,128)}), f32[32,256,128]{2,1,0:T(8,128)}, u32[]{:S(2)}, u32[]{:S(2)}) %all-to-all-start) | async-done | bytes 4194336 | tf_op jit(solution)/shard_map/all_to_all | solution.py:29
  121.0 45.7 %scatter_custom_fusion.1 = f32[4096,128]{1,0:T(8,128)} fusion(s32[8192]{0:T(1024)S(1)} %bitcast.60, f32[8192,128]{1,0:T(8,128)} %bitcast.4, f32[]{:T(128)} %constant.0.clone.1), kind=kCustom, calls=%fused_computation.21 | custom fusion | flops 1048576 | bytes 2097664 | tf_op jit(solution)/shard_map/scatter-add | solution.py:35
  166.7 0.0 all-reduce.5.cloned.1.call-update
  166.8 0.0 all-reduce.7.cloned.1.call-start
  166.8 59.8 %all-reduce.5.cloned.1.call-done = f32[4096,128]{1,0:T(8,128)} async-done(((f32[4096,128]{1,0:T(8,128)}), f32[4096,128]{1,0:T(8,128)}) %all-reduce.5.cloned.1.call-update) | async-done | bytes 2097168 | tf_op jit(solution)/shard_map/psum | solution.py:37
  226.6 0.0 copy-done
  226.6 0.0 copy-done.5
  226.6 4.0 fusion.1
  230.6 4.8 fusion.15
  235.4 0.0 all-reduce.7.cloned.1.call-update
  235.4 0.0 all-reduce.9.cloned.1.call-start
  235.5 58.7 %all-reduce.7.cloned.1.call-done = f32[4096,128]{1,0:T(8,128)} async-done(((f32[4096,128]{1,0:T(8,128)}), f32[4096,128]{1,0:T(8,128)}) %all-reduce.7.cloned.1.call-update) | async-done | bytes 2097168 | tf_op jit(solution)/shard_map/psum | solution.py:42
  294.2 29.3 %gather_fusion.1 = f32[8192,128]{1,0:T(8,128)} fusion(f32[4096,128]{1,0:T(8,128)} %all-reduce.7.cloned.1.call-done, s32[8192]{0:T(1024)S(1)} %broadcast_clamp_fusion), kind=kCustom, calls=%fused_computation.1 | custom fusion | bytes 8421376 | tf_op jit(solution)/shard_map/gather | solution.py:45
  323.5 0.0 copy-start.2
  323.5 58.7 %all_to_all.20 = f32[32,256,128]{2,1,0:T(8,128)S(1)} all-to-all(f32[32,256,128]{2,1,0:T(8,128)} %bitcast.51), channel_id=1, replica_groups=mesh['space'=32,'shell'=4] {'space'}, dimensions={0} | all-to-all | bytes 8388608 | tf_op jit(solution)/shard_map/all_to_all | solution.py:47
  382.2 0.0 copy-done.2
  382.2 3.7 multiply_reduce_fusion.2
  385.9 43.7 %scatter_custom_fusion.2 = f32[2048]{0:T(1024)S(1)} fusion(s32[8192]{0:T(1024)S(1)} %bitcast.57, f32[8192]{0:T(1024)S(1)} %bitcast.66, f32[]{:T(128)} %constant.0.clone.1), kind=kCustom, calls=%fused_computation.33 | custom fusion | flops 8192 | bytes 8196 | tf_op jit(solution)/shard_map/scatter-add | solution.py:50
  429.6 43.5 %scatter_custom_fusion = f32[2048]{0:T(1024)S(1)} fusion(s32[8192]{0:T(1024)S(1)} %bitcast.58, f32[8192]{0:T(1024)S(1)} %bitcast.64, f32[]{:T(128)} %constant.5.clone.1), kind=kCustom, calls=%fused_computation.36 | custom fusion | flops 8192 | bytes 8196 | tf_op jit(solution)/shard_map/scatter-add | solution.py:22
  473.2 45.5 %gather_fusion.2 = f32[8192]{0:T(1024)S(1)} fusion(f32[2048]{0:T(1024)S(1)} %subtract_maximum_fusion.1, s32[8192]{0:T(1024)S(1)} %broadcast_clamp_fusion.1), kind=kCustom, calls=%fused_computation.2 | custom fusion | bytes 98304 | tf_op jit(solution)/shard_map/gather | solution.py:28
  518.8 6.1 fusion.2
  524.8 54.7 %all_to_all.21 = f32[32,256,128]{2,1,0:T(8,128)} all-to-all(f32[32,256,128]{2,1,0:T(8,128)S(1)} %fusion.2), channel_id=1, replica_groups=mesh['space'=32,'shell'=4] {'space'}, dimensions={0} | all-to-all | bytes 8388608 | tf_op jit(solution)/shard_map/all_to_all | solution.py:29
  579.6 45.7 %scatter_custom_fusion.3 = f32[4096,128]{1,0:T(8,128)} fusion(s32[8192]{0:T(1024)S(1)} %bitcast.62, f32[8192,128]{1,0:T(8,128)} %bitcast.52, f32[]{:T(128)} %constant.0.clone.1), kind=kCustom, calls=%fused_computation.19 | custom fusion | flops 1048576 | bytes 2097664 | tf_op jit(solution)/shard_map/scatter-add | solution.py:35
  625.3 0.0 all-reduce.9.cloned.1.call-update
  625.3 0.0 all-reduce.11.cloned.1.call-start
  625.4 55.9 %all-reduce.9.cloned.1.call-done = f32[4096,128]{1,0:T(8,128)} async-done(((f32[4096,128]{1,0:T(8,128)}), f32[4096,128]{1,0:T(8,128)}) %all-reduce.9.cloned.1.call-update) | async-done | bytes 2097168 | tf_op jit(solution)/shard_map/psum | solution.py:37
  681.3 4.0 fusion
  685.2 0.0 copy-start.4
  685.2 4.8 fusion.16
  690.0 0.0 all-reduce.11.cloned.1.call-update
  690.1 58.8 %all-reduce.11.cloned.1.call-done = f32[4096,128]{1,0:T(8,128)} async-done(((f32[4096,128]{1,0:T(8,128)}), f32[4096,128]{1,0:T(8,128)}) %all-reduce.11.cloned.1.call-update) | async-done | bytes 2097168 | tf_op jit(solution)/shard_map/psum | solution.py:42
  748.8 29.3 %gather_fusion.3 = f32[8192,128]{1,0:T(8,128)} fusion(f32[4096,128]{1,0:T(8,128)} %all-reduce.11.cloned.1.call-done, s32[8192]{0:T(1024)S(1)} %broadcast_clamp_fusion), kind=kCustom, calls=%fused_computation.3 | custom fusion | bytes 8421376 | tf_op jit(solution)/shard_map/gather | solution.py:45
  778.1 0.0 copy-done.4
  778.1 0.0 copy-start.3
  778.1 58.7 %all_to_all.22 = f32[32,256,128]{2,1,0:T(8,128)S(1)} all-to-all(f32[32,256,128]{2,1,0:T(8,128)} %bitcast.50), channel_id=1, replica_groups=mesh['space'=32,'shell'=4] {'space'}, dimensions={0} | all-to-all | bytes 8388608 | tf_op jit(solution)/shard_map/all_to_all | solution.py:47
  836.8 0.0 copy-done.3
  836.8 2.7 multiply_reduce_fusion
  839.5 43.5 %scatter_custom_fusion.4 = f32[2048]{0:T(1024)S(1)} fusion(s32[8192]{0:T(1024)S(1)} %bitcast.59, f32[8192]{0:T(1024)S(1)} %bitcast.65, f32[]{:T(128)} %constant.0.clone.1), kind=kCustom, calls=%fused_computation.31 | custom fusion | flops 8192 | bytes 8196 | tf_op jit(solution)/shard_map/scatter-add | solution.py:50
  883.0 0.6 subtract_maximum_fusion
  (11 shorter events, 0.2 us)
Async XLA Ops:
  7.2 219.4 %copy-start = (f32[128,64]{0,1:T(8,128)S(1)}, f32[128,64]{0,1:T(8,128)}, u32[]{:S(2)}) copy-start(f32[128,64]{0,1:T(8,128)} %param.12) | copy-start | bytes 98308
  7.2 1.6 copy-start.1
  62.0 8.8 copy-start.6
  62.0 59.0 %all-to-all-start = ((f32[32,256,128]{2,1,0:T(8,128)}), f32[32,256,128]{2,1,0:T(8,128)}, u32[]{:S(2)}, u32[]{:S(2)}) async-start(f32[32,256,128]{2,1,0:T(8,128)} %fusion.3), calls=%async_computation | async-start | bytes 8388608 | tf_op jit(solution)/shard_map/all_to_all | solution.py:29
  70.7 155.8 %copy-start.5 = (f32[64,4096]{1,0:T(8,128)S(1)}, f32[64,4096]{1,0:T(8,128)}, u32[]{:S(2)}) copy-start(f32[64,4096]{1,0:T(8,128)} %param.13) | copy-start | bytes 3145732
  70.8 155.8 %all-reduce.5.cloned.1.call-start = ((), (), s32[]{:S(2)}) async-start(), calls=%async_computation.4 | async-start | bytes 4194304 | tf_op jit(solution)/shard_map/psum | solution.py:37
  166.8 127.4 %all-reduce.7.cloned.1.call-start = ((), (), s32[]{:S(2)}) async-start(), calls=%async_computation.5 | async-start | bytes 4194304 | tf_op jit(solution)/shard_map/psum | solution.py:42
  235.4 445.8 %all-reduce.9.cloned.1.call-start = ((), (), s32[]{:S(2)}) async-start(), calls=%async_computation.6 | async-start | bytes 4194304 | tf_op jit(solution)/shard_map/psum | solution.py:37
  323.5 58.7 %copy-start.2 = (f32[1,1,32,256,128]{4,3,2,1,0:T(8,128)S(1)}, f32[1,1,32,256,128]{4,3,2,1,0:T(8,128)}, u32[]{:S(2)}) copy-start(f32[1,1,32,256,128]{4,3,2,1,0:T(8,128)} %param.9) | copy-start | bytes 12582916
  625.3 123.5 %all-reduce.11.cloned.1.call-start = ((), (), s32[]{:S(2)}) async-start(), calls=%async_computation.7 | async-start | bytes 4194304 | tf_op jit(solution)/shard_map/psum | solution.py:42
  685.2 92.9 %copy-start.4 = (f32[64,4096]{1,0:T(8,128)}, f32[64,4096]{1,0:T(8,128)S(1)}, u32[]{:S(2)}) copy-start(f32[64,4096]{1,0:T(8,128)S(1)} %fusion) | copy-start | bytes 3145732
  778.1 58.7 %copy-start.3 = (f32[1,1,32,256,128]{4,3,2,1,0:T(8,128)S(1)}, f32[1,1,32,256,128]{4,3,2,1,0:T(8,128)}, u32[]{:S(2)}) copy-start(f32[1,1,32,256,128]{4,3,2,1,0:T(8,128)} %param.9) | copy-start | bytes 12582916
Sparse Core Ops, SparseCore 0:
  166.9 59.6 all-reduce.4
  235.5 58.6 all-reduce.6
  625.4 55.7 all-reduce.8
  690.2 58.6 all-reduce.10
where the time goes:
time: 891 us; the launch traced here: 890 us
  waiting for transfers between devices  283 us (32%)
  other arithmetic  244 us (27%)
  blocking collectives  172 us (19%)
  local copies, waits for them, and re-layouts  150 us (17%)
  matrix products  17.6 us (2%)
  between operations  14 us (2%)
  starting transfers between devices  8.94 us (1%)
    psum x2, waiting for transfers between devices, on_device(): lax.psum(jnp.einsum('gv,jg->vj', residual, dictionary, precision=lax.Prec...  118 us
    all_to_all x2, blocking collectives, on_device(): lax.all_to_all(adj_rows, 'space', split_axis=0, concat_axis=0, tiled=True)  117 us
    psum x2, waiting for transfers between devices, on_device(): coeff_sum = lax.psum(partial_coeff, 'shell')  116 us
    scatter-add x2, other arithmetic, on_device(): partial_coeff = jnp.zeros((voxel_count, coeffs), jnp.float32).at[voxel_in...  91.4 us
    gather x4, local copies, waits for them, and re-layouts, on_device(): picked = current[stream_index]  91.1 us
    scatter-add x2, other arithmetic, on_device(): jnp.zeros(weights.shape, jnp.float32).at[stream_index].add(grad_slot)  87.2 us
    gather x2, local copies, waits for them, and re-layouts, on_device(): adj_rows = adjoint[voxel_index].reshape(blocks, slots, coeffs)  58.6 us
    all_to_all x1, blocking collectives, on_device(): lax.all_to_all(picked[:, :, None] * masked, 'space', split_axis=0, concat...  54.7 us
  transfers between devices with their start and end apart: 5, of which 5 were waited for; matrix products, arithmetic and copies ran while one was open for 0% of the time, Pallas kernels for 0%

commit v1 on v0

--- a/solution.py
+++ b/solution.py
@@ -34,7 +34,7 @@
             .at[voxel_index]
             .add(seg_terms.reshape(blocks * slots, coeffs))
         )
-        coeff_sum = lax.psum(partial_coeff, "shell")
+        coeff_sum = jnp.sum(lax.all_gather(partial_coeff, "shell"), axis=0)
         residual = (
             jnp.einsum("jg,vj->gv", dictionary, coeff_sum, precision=lax.Precision.HIGHEST)
             - measured

time: 891 us -> 948 us (1.064)
  waiting for transfers between devices: 283 us -> 334 us
    all_gather x0 -> x2, waiting for transfers between devices: none -> 164 us  [on_device(): coeff_sum = jnp.sum(lax.all_gather(partial_coeff, 'shell'), axis=0)]
    psum x2 -> x0, waiting for transfers between devices: 116 us -> none  [on_device(): coeff_sum = lax.psum(partial_coeff, 'shell')]
where the time goes in v1:
time: 948 us; the launch traced here: 947 us
  waiting for transfers between devices  334 us (35%)
  other arithmetic  252 us (27%)
  blocking collectives  172 us (18%)
  local copies, waits for them, and re-layouts  150 us (16%)
  matrix products  15.7 us (2%)
  between operations  14 us (1%)
    all_gather x2, waiting for transfers between devices, on_device(): coeff_sum = jnp.sum(lax.all_gather(partial_coeff, 'shell'), axis=0)  164 us
    psum x2, waiting for transfers between devices, on_device(): lax.psum(jnp.einsum('gv,jg->vj', residual, dictionary, precision=lax.Prec...  120 us
    all_to_all x2, blocking collectives, on_device(): lax.all_to_all(adj_rows, 'space', split_axis=0, concat_axis=0, tiled=True)  117 us
    scatter-add x2, other arithmetic, on_device(): partial_coeff = jnp.zeros((voxel_count, coeffs), jnp.float32).at[voxel_in...  91.6 us
    gather x4, local copies, waits for them, and re-layouts, on_device(): picked = current[stream_index]  91.1 us
    scatter-add x2, other arithmetic, on_device(): jnp.zeros(weights.shape, jnp.float32).at[stream_index].add(grad_slot)  87.1 us
    gather x2, local copies, waits for them, and re-layouts, on_device(): adj_rows = adjoint[voxel_index].reshape(blocks, slots, coeffs)  58.6 us
    all_to_all x1, blocking collectives, on_device(): lax.all_to_all(picked[:, :, None] * masked, 'space', split_axis=0, concat...  54.7 us
  transfers between devices with their start and end apart: 5, of which 5 were waited for; matrix products, arithmetic and copies ran while one was open for 0% of the time, Pallas kernels for 0%

profile of v1, /device:TPU:1, one launch (start us, length us, event | category | flops | bytes accessed | tf_op | source)
XLA Modules:
  0.0 946.9 jit_solution(1805187643274975490)
XLA Ops:
  7.2 0.0 copy-start
  7.2 0.0 copy-start.1
  7.2 0.8 fusion.8
  8.0 0.0 copy-done.1
  8.0 0.0 copy-start.7
  8.0 45.5 %gather_fusion = f32[8192]{0:T(1024)S(1)} fusion(f32[2048]{0:T(1024)S(1)} %copy-done.1, s32[8192]{0:T(1024)S(1)} %broadcast_clamp_fusion.1), kind=kCustom, calls=%fused_computation | custom fusion | bytes 98304 | tf_op jit(solution)/shard_map/gather | solution.py:28
  53.6 0.0 copy-done.7
  53.6 0.1 iota_compare_fusion
  53.7 7.7 fusion.3
  61.3 0.0 copy-start.6
  61.3 8.8 all-to-all-start
  70.1 0.0 all-gather.5.cloned.1.call-start
  70.2 0.0 copy-done.6
  70.3 50.1 %all-to-all-done = f32[32,256,128]{2,1,0:T(8,128)} async-done(((f32[32,256,128]{2,1,0:T(8,128)}), f32[32,256,128]{2,1,0:T(8,128)}, u32[]{:S(2)}, u32[]{:S(2)}) %all-to-all-start) | async-done | bytes 4194336 | tf_op jit(solution)/shard_map/all_to_all | solution.py:29
  120.4 45.8 %scatter_custom_fusion.1 = f32[4096,128]{1,0:T(8,128)} fusion(s32[8192]{0:T(1024)S(1)} %bitcast.64, f32[8192,128]{1,0:T(8,128)} %bitcast.4, f32[]{:T(128)} %constant.0.clone.1), kind=kCustom, calls=%fused_computation.21 | custom fusion | flops 1048576 | bytes 2097664 | tf_op jit(solution)/shard_map/scatter-add | solution.py:35
  166.2 0.0 all-gather.5.cloned.1.call-update
  166.2 0.0 all-reduce.3.cloned.1.call-start
  166.2 84.1 %all-gather.5.cloned.1.call-done = f32[16384,128]{1,0:T(8,128)} async-done(((f32[4096,128]{1,0:T(8,128)}), f32[16384,128]{1,0:T(8,128)}) %all-gather.5.cloned.1.call-update) | async-done | bytes 8388624 | tf_op jit(solution)/shard_map/all_gather | solution.py:37
  250.3 0.0 copy-start.5
  250.3 4.2 reduce_sum.46
  254.5 0.0 copy-done
  254.5 0.0 copy-done.5
  254.5 2.4 fusion.1
  256.9 4.8 fusion.15
  261.8 0.0 all-reduce.3.cloned.1.call-update
  261.8 0.0 all-gather.7.cloned.1.call-start
  261.9 59.9 %all-reduce.3.cloned.1.call-done = f32[4096,128]{1,0:T(8,128)} async-done(((f32[4096,128]{1,0:T(8,128)}), f32[4096,128]{1,0:T(8,128)}) %all-reduce.3.cloned.1.call-update) | async-done | bytes 2097168 | tf_op jit(solution)/shard_map/psum | solution.py:42
  321.8 29.3 %gather_fusion.1 = f32[8192,128]{1,0:T(8,128)} fusion(f32[4096,128]{1,0:T(8,128)} %all-reduce.3.cloned.1.call-done, s32[8192]{0:T(1024)S(1)} %broadcast_clamp_fusion), kind=kCustom, calls=%fused_computation.1 | custom fusion | bytes 8421376 | tf_op jit(solution)/shard_map/gather | solution.py:45
  351.0 0.0 copy-start.2
  351.0 58.7 %all_to_all.20 = f32[32,256,128]{2,1,0:T(8,128)S(1)} all-to-all(f32[32,256,128]{2,1,0:T(8,128)} %bitcast.53), channel_id=1, replica_groups=mesh['space'=32,'shell'=4] {'space'}, dimensions={0} | all-to-all | bytes 8388608 | tf_op jit(solution)/shard_map/all_to_all | solution.py:47
  409.7 0.0 copy-done.2
  409.7 3.7 multiply_reduce_fusion.2
  413.5 43.5 %scatter_custom_fusion.2 = f32[2048]{0:T(1024)S(1)} fusion(s32[8192]{0:T(1024)S(1)} %bitcast.61, f32[8192]{0:T(1024)S(1)} %bitcast.70, f32[]{:T(128)} %constant.0.clone.1), kind=kCustom, calls=%fused_computation.33 | custom fusion | flops 8192 | bytes 8196 | tf_op jit(solution)/shard_map/scatter-add | solution.py:50
  457.0 43.5 %scatter_custom_fusion = f32[2048]{0:T(1024)S(1)} fusion(s32[8192]{0:T(1024)S(1)} %bitcast.62, f32[8192]{0:T(1024)S(1)} %bitcast.68, f32[]{:T(128)} %constant.5.clone.1), kind=kCustom, calls=%fused_computation.36 | custom fusion | flops 8192 | bytes 8196 | tf_op jit(solution)/shard_map/scatter-add | solution.py:22
  500.6 45.5 %gather_fusion.2 = f32[8192]{0:T(1024)S(1)} fusion(f32[2048]{0:T(1024)S(1)} %subtract_maximum_fusion.1, s32[8192]{0:T(1024)S(1)} %broadcast_clamp_fusion.1), kind=kCustom, calls=%fused_computation.2 | custom fusion | bytes 98304 | tf_op jit(solution)/shard_map/gather | solution.py:28
  546.1 6.1 fusion.2
  552.2 54.7 %all_to_all.21 = f32[32,256,128]{2,1,0:T(8,128)} all-to-all(f32[32,256,128]{2,1,0:T(8,128)S(1)} %fusion.2), channel_id=1, replica_groups=mesh['space'=32,'shell'=4] {'space'}, dimensions={0} | all-to-all | bytes 8388608 | tf_op jit(solution)/shard_map/all_to_all | solution.py:29
  606.9 45.8 %scatter_custom_fusion.3 = f32[4096,128]{1,0:T(8,128)} fusion(s32[8192]{0:T(1024)S(1)} %bitcast.66, f32[8192,128]{1,0:T(8,128)} %bitcast.56, f32[]{:T(128)} %constant.0.clone.1), kind=kCustom, calls=%fused_computation.19 | custom fusion | flops 1048576 | bytes 2097664 | tf_op jit(solution)/shard_map/scatter-add | solution.py:35
  652.7 0.0 all-gather.7.cloned.1.call-update
  652.7 0.3 all-reduce.5.cloned.1.call-start
  653.0 80.0 %all-gather.7.cloned.1.call-done = f32[16384,128]{1,0:T(8,128)} async-done(((f32[4096,128]{1,0:T(8,128)}), f32[16384,128]{1,0:T(8,128)}) %all-gather.7.cloned.1.call-update) | async-done | bytes 8388624 | tf_op jit(solution)/shard_map/all_gather | solution.py:37
  733.0 4.1 reduce_sum.48
  737.1 3.6 fusion
  740.7 0.0 copy-start.4
  740.8 4.8 fusion.16
  745.5 0.0 all-reduce.5.cloned.1.call-update
  745.6 60.0 %all-reduce.5.cloned.1.call-done = f32[4096,128]{1,0:T(8,128)} async-done(((f32[4096,128]{1,0:T(8,128)}), f32[4096,128]{1,0:T(8,128)}) %all-reduce.5.cloned.1.call-update) | async-done | bytes 2097168 | tf_op jit(solution)/shard_map/psum | solution.py:42
  805.6 29.3 %gather_fusion.3 = f32[8192,128]{1,0:T(8,128)} fusion(f32[4096,128]{1,0:T(8,128)} %all-reduce.5.cloned.1.call-done, s32[8192]{0:T(1024)S(1)} %broadcast_clamp_fusion), kind=kCustom, calls=%fused_computation.3 | custom fusion | bytes 8421376 | tf_op jit(solution)/shard_map/gather | solution.py:45
  834.8 0.0 copy-done.4
  834.8 0.0 copy-start.3
  834.8 58.7 %all_to_all.22 = f32[32,256,128]{2,1,0:T(8,128)S(1)} all-to-all(f32[32,256,128]{2,1,0:T(8,128)} %bitcast.52), channel_id=1, replica_groups=mesh['space'=32,'shell'=4] {'space'}, dimensions={0} | all-to-all | bytes 8388608 | tf_op jit(solution)/shard_map/all_to_all | solution.py:47
  893.5 0.0 copy-done.3
  893.5 2.7 multiply_reduce_fusion
  896.2 43.5 %scatter_custom_fusion.4 = f32[2048]{0:T(1024)S(1)} fusion(s32[8192]{0:T(1024)S(1)} %bitcast.63, f32[8192]{0:T(1024)S(1)} %bitcast.69, f32[]{:T(128)} %constant.0.clone.1), kind=kCustom, calls=%fused_computation.31 | custom fusion | flops 8192 | bytes 8196 | tf_op jit(solution)/shard_map/scatter-add | solution.py:50
  939.7 0.6 subtract_maximum_fusion
  (11 shorter events, 0.2 us)
Async XLA Ops:
  7.2 247.3 %copy-start = (f32[128,64]{0,1:T(8,128)S(1)}, f32[128,64]{0,1:T(8,128)}, u32[]{:S(2)}) copy-start(f32[128,64]{0,1:T(8,128)} %param.12) | copy-start | bytes 98308
  7.2 0.8 copy-start.1
  8.0 45.6 %copy-start.7 = (s32[1,1,32]{2,1,0:T(1,128)S(1)}, s32[1,1,32]{2,1,0:T(1,128)}, u32[]{:S(2)}) copy-start(s32[1,1,32]{2,1,0:T(1,128)} %param.10) | copy-start | bytes 388
  61.3 8.8 copy-start.6
  61.3 59.1 %all-to-all-start = ((f32[32,256,128]{2,1,0:T(8,128)}), f32[32,256,128]{2,1,0:T(8,128)}, u32[]{:S(2)}, u32[]{:S(2)}) async-start(f32[32,256,128]{2,1,0:T(8,128)} %fusion.3), calls=%async_computation | async-start | bytes 8388608 | tf_op jit(solution)/shard_map/all_to_all | solution.py:29
  70.1 180.2 %all-gather.5.cloned.1.call-start = ((), (), s32[]{:S(2)}) async-start(), calls=%async_computation.6 | async-start | bytes 10485760 | tf_op jit(solution)/shard_map/all_gather | solution.py:37
  166.2 155.6 %all-reduce.3.cloned.1.call-start = ((), (), s32[]{:S(2)}) async-start(), calls=%async_computation.4 | async-start | bytes 4194304 | tf_op jit(solution)/shard_map/psum | solution.py:42
  250.3 4.2 copy-start.5
  261.8 471.3 %all-gather.7.cloned.1.call-start = ((), (), s32[]{:S(2)}) async-start(), calls=%async_computation.7 | async-start | bytes 10485760 | tf_op jit(solution)/shard_map/all_gather | solution.py:37
  351.0 58.7 %copy-start.2 = (f32[1,1,32,256,128]{4,3,2,1,0:T(8,128)S(1)}, f32[1,1,32,256,128]{4,3,2,1,0:T(8,128)}, u32[]{:S(2)}) copy-start(f32[1,1,32,256,128]{4,3,2,1,0:T(8,128)} %param.9) | copy-start | bytes 12582916
  652.7 152.8 %all-reduce.5.cloned.1.call-start = ((), (), s32[]{:S(2)}) async-start(), calls=%async_computation.5 | async-start | bytes 4194304 | tf_op jit(solution)/shard_map/psum | solution.py:42
  740.7 94.1 %copy-start.4 = (f32[64,4096]{1,0:T(8,128)}, f32[64,4096]{1,0:T(8,128)S(1)}, u32[]{:S(2)}) copy-start(f32[64,4096]{1,0:T(8,128)S(1)} %fusion) | copy-start | bytes 3145732
  834.8 58.7 %copy-start.3 = (f32[1,1,32,256,128]{4,3,2,1,0:T(8,128)S(1)}, f32[1,1,32,256,128]{4,3,2,1,0:T(8,128)}, u32[]{:S(2)}) copy-start(f32[1,1,32,256,128]{4,3,2,1,0:T(8,128)} %param.9) | copy-start | bytes 12582916
Sparse Core Ops, SparseCore 0:
  166.3 83.9 all-gather.4
  261.9 59.8 all-reduce.2
  652.9 80.1 all-gather.6
  745.7 59.8 all-reduce.4
